TPU v7x, 256 devices: a whole 4x4x8 slice. The times are simulated.
256 devices in a mesh: tiles: 64 (over y, z, core), cols: 4 (over x).
Axes of the slice: x: 4, y: 4, z: 8, core: 2. Of those that a mesh axis runs over, the one named last changes fastest.
Arguments:
- cov_blocks: bfloat16 [1024, 8, 256, 256], P('tiles', None, 'cols'), may hold values from -1 to 5, as said below
- neighbours: int32 [1024, 8], P('tiles'), may hold values from 0 to 1023, as said below
- voxel_mask: int32 [1024, 256], P('tiles', 'cols'), may hold values 0 or 1
- start_block: bfloat16 [128, 1024, 256], P('cols', 'tiles'), may hold values from -6 to 6
- overdensity: float32 [1024, 256], P('tiles', 'cols'), may hold values from -12 to 12
Outputs:
- basis_next: bfloat16 [128, 1024, 256], P('cols', 'tiles')
- coeffs: float32 [3, 128], replicated
Inputs may be any that keep to these rules, and one draw needn't show every extreme that they name: Slot 0 names the tile itself. Every other entry names another tile at most 3 away, counting cyclically (tile 1024 - 1 is next to tile 0), and some entry is exactly 3 away. If neighbours[i, k] = j then neighbours[j, k] = i. cov_blocks[j, k] is the transpose of cov_blocks[i, k] where neighbours[i, k] = j; the blocks of slot 0 are symmetric.
All inputs are finite; a program needn't handle non-finite values. No bound on the sum of `voxel_mask` on one device may be relied on, other than what follows from the above.
Results may differ from a plain program's by a relative error of at most 0.01.
The roundings to bfloat16 on the way count: a program that leaves them out, or rounds other values in their place, can miss the bound.
Values may be sent and summed in bfloat16 or wider, within the bound.
No kernel may reach another device: no remote copies, remote signals or barrier semaphores. Data moves between devices by JAX's collectives and lax.ppermute only.
A program may use at most 64 MiB of HBM per device.

v0:
```python
import math
import jax
import jax.numpy as jnp
from jax import lax
from jax.sharding import PartitionSpec as P

REACH = 3


def with_halo(cells, sides, width):
    for axis, dim in sides:
        count = lax.axis_size(axis)
        head = lax.slice_in_dim(cells, 0, width, axis=dim)
        tail = lax.slice_in_dim(cells, cells.shape[dim] - width, cells.shape[dim], axis=dim)
        cells = jnp.concatenate(
            [
                lax.ppermute(tail, axis, [(i, (i + 1) % count) for i in range(count)]),
                cells,
                lax.ppermute(head, axis, [((i + 1) % count, i) for i in range(count)]),
            ],
            axis=dim,
        )
    return cells


def pair_step(x, axis, count, stride):
    perm = [(i, i ^ stride) for i in range(count)]
    return x + lax.ppermute(x, axis, perm)


def group_step(x, axis, count, stride, size):
    me = lax.axis_index(axis) // stride % size
    vals = [x]
    for shift in range(1, size):
        perm = []
        for i in range(count):
            digit = i // stride % size
            perm.append((i, i + ((digit + shift) % size - digit) * stride))
        vals.append(lax.ppermute(x, axis, perm))
    ordered = jnp.take(jnp.stack(vals), (me - jnp.arange(size)) % size, axis=0)
    return jnp.sum(ordered, axis=0)


def plan_of(count):
    stages = []
    stride = 1
    pair_next = count > 4
    while stride < count:
        if not pair_next and count // stride >= 4:
            stages.append(("group", stride, 4))
            stride *= 4
        else:
            stages.append(("pair", stride, 2))
            stride *= 2
        pair_next = not pair_next
    return stages


def all_sum(x, axes=("cols", "tiles")):
    for axis in axes:
        count = lax.axis_size(axis)
        if count & count - 1:
            x = lax.psum(x, axis)
            continue
        for kind, stride, size in plan_of(count):
            if kind == "pair":
                x = pair_step(x, axis, count, stride)
            else:
                x = group_step(x, axis, count, stride, size)
    return x


def orthonormal(work):
    gram = all_sum(jnp.dot(work, work.T, preferred_element_type=jnp.float32))
    lower = jnp.linalg.cholesky(gram)
    identity = jnp.eye(work.shape[0], dtype=jnp.float32)
    inverse = jax.scipy.linalg.solve_triangular(lower, identity, lower=True).astype(jnp.bfloat16)
    return jnp.dot(inverse, work, preferred_element_type=jnp.float32)


def projection(basis_flat, density):
    return jnp.sum(basis_flat.astype(jnp.float32) * density[None, :], axis=1)


def fold_slots(total, piece, cov_blocks, local_index):
    for slot in range(cov_blocks.shape[1]):
        picked = jnp.take(piece, local_index[:, slot], axis=1)
        blocks = cov_blocks[:, slot]
        total = total + jnp.einsum(
            "iuv,biv->biu", blocks, picked, preferred_element_type=jnp.float32
        )
    return total


def local(cov_blocks, neighbours, voxel_mask, start_block, overdensity):
    tiles_here = neighbours.shape[0]
    voxels_here = voxel_mask.shape[1]
    voxels_all = cov_blocks.shape[3]
    cycle_size = tiles_here * lax.axis_size("tiles")
    first_tile = lax.axis_index("tiles") * tiles_here
    local_index = jnp.mod(neighbours - first_tile + REACH, cycle_size)
    mask_values = voxel_mask.astype(jnp.float32)
    density = overdensity.reshape(-1)
    start_cube = lax.all_to_all(start_block, "cols", split_axis=2, concat_axis=0, tiled=True)
    count = start_cube.shape[0]
    start_flat = (
        (start_cube.astype(jnp.float32) * mask_values[None]).astype(jnp.bfloat16).reshape(count, -1)
    )
    basis_now = orthonormal(start_flat).astype(jnp.bfloat16)
    basis_old = None
    found = []
    pending = projection(basis_now, density)
    rotated = None
    for lanczos_round in range(2):
        image_count = basis_now.shape[0]
        basis_cube = basis_now.reshape(image_count, tiles_here, voxels_here)
        empty = jnp.zeros((image_count, tiles_here, voxels_here), jnp.float32)
        gathered = lax.all_gather(basis_cube, "cols", axis=2, tiled=True)
        padded = with_halo(gathered, (("tiles", 1),), REACH)
        total = fold_slots(empty, padded, cov_blocks, local_index)
        image = (total * mask_values[None]).astype(jnp.bfloat16).reshape(image_count, -1)
        if basis_old is None:
            stacked = basis_now
        else:
            stacked = jnp.concatenate([basis_now, basis_old], axis=0)
        local_sums = jnp.dot(stacked, image.T, preferred_element_type=jnp.float32)
        sums = all_sum(jnp.concatenate([local_sums, pending[None]], axis=0))
        found.append(sums[-1])
        along = sums[:count].astype(jnp.bfloat16)
        resid = image.astype(jnp.float32) - jnp.dot(
            along.T, basis_now, preferred_element_type=jnp.float32
        )
        if basis_old is not None:
            back = sums[count : 2 * count].astype(jnp.bfloat16)
            resid = resid - jnp.dot(back.T, basis_old, preferred_element_type=jnp.float32)
        rotated = orthonormal(resid.astype(jnp.bfloat16))
        basis_old, basis_now = (basis_now, rotated.astype(jnp.bfloat16))
        pending = projection(basis_now, density)
    found.append(all_sum(pending))
    coeffs = jnp.stack(found)
    scaled = (rotated * math.sqrt(cycle_size * voxels_all)).astype(jnp.bfloat16)
    scaled = scaled.reshape(count, tiles_here, voxels_here)
    basis_next = lax.all_to_all(scaled, "cols", split_axis=0, concat_axis=2, tiled=True)
    return (basis_next, coeffs)


def solution(mesh):
    return jax.shard_map(
        local,
        mesh=mesh,
        in_specs=(
            P("tiles", None, "cols", None),
            P("tiles", None),
            P("tiles", "cols"),
            P("cols", "tiles", None),
            P("tiles", "cols"),
        ),
        out_specs=(P("cols", "tiles", None), P()),
        check_vma=False,
    )
```

profile of v0, /device:TPU:8, one launch (start us, length us, event | category | flops | bytes accessed | tf_op | source)
XLA Modules:
  0.0 462.4 jit_solution(13479169176730320562)
XLA Ops:
  11.2 4.3 all-to-all-start
  17.1 5.1 %all-to-all-done = bf16[4,2,16384]{2,1,0:T(2,128)(2,1)S(1)} async-done(((bf16[4,2,16384]{2,1,0:T(2,128)(2,1)}), bf16[4,2,16384]{2,1,0:T(2,128)(2,1)S(1)}, u32[]{:S(2)}, u32[]{:S(2)}) %all-to-all-start) | async-done | bytes 262176 | tf_op jit(solution)/shard_map/all_to_all | solution.py:104
  35.3 3.3 collective-permute-start.5
  44.5 5.8 %collective-permute-start.7 = (f32[128,128]{1,0:T(8,128)S(1)}, f32[128,128]{1,0:T(8,128)S(1)}, u32[]{:S(2)}, u32[]{:S(2)}) collective-permute-start(f32[128,128]{1,0:T(8,128)S(1)} %select_reduce_fusion.13), channel_id=1, source_target_pairs={{0,32},{4,36},{8,40},{12,44},{16,48},{20,52},{24,56},{28,60},{32,0... | collective-permute-start | bytes 196616 | tf_op jit(solution)/shard_map/ppermute | solution.py:28
  55.3 2.6 collective-permute-start.10
  61.3 11.7 %cholesky.59 = f32[128,128]{1,0:T(8,128)S(1)} custom-call(f32[128,128]{1,0:T(8,128)S(1)} %fusion.122), custom_call_target="Cholesky" | custom-call | tf_op jit(solution)/shard_map/jit(cholesky)/cholesky | solution.py:75
  74.3 9.8 %custom-call.7 = f32[1,128,128]{1,2,0:T(8,128)S(1)} custom-call(f32[1,128,128]{2,1,0:T(8,128)S(1)} %fusion.114), custom_call_target="InvertDiagBlocksLowerTriangular" | custom-call | tf_op jit(solution)/shard_map/jit(_solve_triangular)/triangular_solve | solution.py:77
  85.9 29.2 %all-gather.3.cloned.1.call-done = bf16[128,16,256]{0,1,2:T(8,128)(2,1)} async-done(((bf16[128,16,64]{0,1,2:T(8,128)(2,1)}), bf16[128,16,256]{0,1,2:T(8,128)(2,1)}) %all-gather.3.cloned.1.call-update) | async-done | bytes 1048592 | tf_op jit(solution)/shard_map/all_gather | solution.py:118
  116.9 4.0 collective-permute-start.12
  120.9 3.1 collective-permute-done.11
  145.6 2.7 collective-permute-start.14
  154.9 4.1 collective-permute-start.18
  159.0 2.7 collective-permute-done.17
  161.7 2.5 collective-permute-done.18
  165.2 4.1 collective-permute-start.20
  169.3 4.9 %collective-permute-done.20 = f32[129,128]{1,0:T(8,128)S(1)} collective-permute-done((f32[129,128]{1,0:T(8,128)S(1)}, f32[129,128]{1,0:T(8,128)S(1)}, u32[]{:S(2)}, u32[]{:S(2)}) %collective-permute-start.20) | collective-permute-done | bytes 66080 | tf_op jit(solution)/shard_map/ppermute | solution.py:28
  185.2 2.8 collective-permute-start.25
  198.3 2.8 collective-permute-done.28
  203.9 3.9 collective-permute-start.31
  207.8 5.1 %collective-permute-done.31 = f32[128,128]{1,0:T(8,128)S(1)} collective-permute-done((f32[128,128]{1,0:T(8,128)S(1)}, f32[128,128]{1,0:T(8,128)S(1)}, u32[]{:S(2)}, u32[]{:S(2)}) %collective-permute-start.31) | collective-permute-done | bytes 65568 | tf_op jit(solution)/shard_map/ppermute | solution.py:28
  222.2 11.7 %cholesky.70 = f32[128,128]{1,0:T(8,128)S(1)} custom-call(f32[128,128]{1,0:T(8,128)S(1)} %fusion.120), custom_call_target="Cholesky" | custom-call | tf_op jit(solution)/shard_map/jit(cholesky)/cholesky | solution.py:75
  235.3 9.8 %custom-call.8 = f32[1,128,128]{1,2,0:T(8,128)S(1)} custom-call(f32[1,128,128]{2,1,0:T(8,128)S(1)} %fusion.115), custom_call_target="InvertDiagBlocksLowerTriangular" | custom-call | tf_op jit(solution)/shard_map/jit(_solve_triangular)/triangular_solve | solution.py:77
  246.8 24.3 %all-gather.5.cloned.1.call-done = bf16[128,16,256]{0,1,2:T(8,128)(2,1)} async-done(((bf16[128,16,64]{0,1,2:T(8,128)(2,1)}), bf16[128,16,256]{0,1,2:T(8,128)(2,1)}) %all-gather.5.cloned.1.call-update) | async-done | bytes 1048592 | tf_op jit(solution)/shard_map/all_gather | solution.py:118
  272.8 4.0 collective-permute-start.36
  276.9 3.2 collective-permute-done.35
  301.6 2.7 collective-permute-start.38
  306.0 4.9 %collective-permute-done.37 = f32[257,128]{1,0:T(8,128)S(1)} collective-permute-done((f32[257,128]{1,0:T(8,128)S(1)}, f32[257,128]{1,0:T(8,128)S(1)}, u32[]{:S(2)}, u32[]{:S(2)}) %collective-permute-start.37) | collective-permute-done | bytes 131616 | tf_op jit(solution)/shard_map/ppermute | solution.py:39
  313.9 2.6 collective-permute-start.42
  317.8 4.3 collective-permute-done.41
  322.1 4.9 %collective-permute-done.42 = f32[257,128]{1,0:T(8,128)S(1)} collective-permute-done((f32[257,128]{1,0:T(8,128)S(1)}, f32[257,128]{1,0:T(8,128)S(1)}, u32[]{:S(2)}, u32[]{:S(2)}) %collective-permute-start.42) | collective-permute-done | bytes 131616 | tf_op jit(solution)/shard_map/ppermute | solution.py:39
  327.8 5.0 %collective-permute-start.44 = (f32[257,128]{1,0:T(8,128)S(1)}, f32[257,128]{1,0:T(8,128)S(1)}, u32[]{:S(2)}, u32[]{:S(2)}) collective-permute-start(f32[257,128]{1,0:T(8,128)S(1)} %select_reduce_fusion.1), channel_id=1, source_target_pairs={{0,32},{4,36},{8,40},{12,44},{16,48},{20,52},{24,56},{28,60},{32,0... | collective-permute-start | bytes 394760 | tf_op jit(solution)/shard_map/ppermute | solution.py:28
  332.8 4.1 collective-permute-done.44
  339.6 2.5 collective-permute-start.47
  342.3 2.8 collective-permute-done.46
  349.6 2.7 collective-permute-start.49
  358.6 6.5 %collective-permute-start.52 = (f32[128,128]{1,0:T(8,128)S(1)}, f32[128,128]{1,0:T(8,128)S(1)}, u32[]{:S(2)}, u32[]{:S(2)}) collective-permute-start(f32[128,128]{1,0:T(8,128)S(1)} %add.231), channel_id=1, source_target_pairs={{0,8},{4,12},{8,16},{12,20},{16,24},{20,28},{24,0},{28,4},{32,40},... | collective-permute-start | bytes 196616 | tf_op jit(solution)/shard_map/ppermute | solution.py:39
  367.6 3.6 collective-permute-done.53
  371.9 4.2 collective-permute-start.55
  376.1 4.0 collective-permute-done.55
  388.5 11.7 %cholesky.81 = f32[128,128]{1,0:T(8,128)S(1)} custom-call(f32[128,128]{1,0:T(8,128)S(1)} %fusion.118), custom_call_target="Cholesky" | custom-call | tf_op jit(solution)/shard_map/jit(cholesky)/cholesky | solution.py:75
  401.5 9.8 %custom-call.9 = f32[1,128,128]{1,2,0:T(8,128)S(1)} custom-call(f32[1,128,128]{2,1,0:T(8,128)S(1)} %fusion.116), custom_call_target="InvertDiagBlocksLowerTriangular" | custom-call | tf_op jit(solution)/shard_map/jit(_solve_triangular)/triangular_solve | solution.py:77
  412.0 2.7 collective-permute-start.60
  420.2 3.0 collective-permute-start.63
  428.3 4.9 %collective-permute-start.66 = (f32[128]{0:T(128)S(1)}, f32[128]{0:T(128)S(1)}, u32[]{:S(2)}, u32[]{:S(2)}) collective-permute-start(f32[128]{0:T(128)S(1)} %select_reduce_fusion.17), channel_id=1, source_target_pairs={{0,32},{4,36},{8,40},{12,44},{16,48},{20,52},{24,56},{28,60},{32,0... | collective-permute-start | bytes 1544 | tf_op jit(solution)/shard_map/ppermute | solution.py:28
  433.2 2.6 collective-permute-done.66
  436.7 2.8 collective-permute-start.68
  443.0 3.9 all-to-all-start.1
  448.2 5.4 %all-to-all-done.1 = bf16[4,2,16384]{2,1,0:T(2,128)(2,1)S(1)} async-done(((bf16[4,2,16384]{2,1,0:T(2,128)(2,1)}), bf16[4,2,16384]{2,1,0:T(2,128)(2,1)S(1)}, u32[]{:S(2)}, u32[]{:S(2)}) %all-to-all-start.1) | async-done | bytes 262176 | tf_op jit(solution)/shard_map/all_to_all | solution.py:143
  (309 shorter events, 177.9 us)
Async XLA Ops:
  11.2 11.0 %all-to-all-start = ((bf16[4,2,16384]{2,1,0:T(2,128)(2,1)}), bf16[4,2,16384]{2,1,0:T(2,128)(2,1)S(1)}, u32[]{:S(2)}, u32[]{:S(2)}) async-start(bf16[4,2,16384]{2,1,0:T(2,128)(2,1)} %reshape.448), calls=%async_computation | async-start | bytes 524288 | tf_op jit(solution)/shard_map/all_to_all | solution.py:104
  15.5 99.6 %all-gather.3.cloned.1.call-start = ((), (), s32[]{:S(2)}) async-start(), calls=%async_computation.2 | async-start | bytes 1310720 | tf_op jit(solution)/shard_map/all_gather | solution.py:118
  24.2 5.6 %collective-permute-start = (f32[128,128]{1,0:T(8,128)S(1)}, f32[128,128]{1,0:T(8,128)S(1)}, u32[]{:S(2)}, u32[]{:S(2)}) collective-permute-start(f32[128,128]{1,0:T(8,128)S(1)} %bitcast.312), channel_id=1, source_target_pairs={{0,1},{1,2},{2,3},{3,0},{4,5},{5,6},{6,7},{7,4},{8,9},{9,10},{10,1... | collective-permute-start | bytes 196616 | tf_op jit(solution)/shard_map/ppermute | solution.py:39
  24.8 5.8 %collective-permute-start.1 = (f32[128,128]{1,0:T(8,128)S(1)}, f32[128,128]{1,0:T(8,128)S(1)}, u32[]{:S(2)}, u32[]{:S(2)}) collective-permute-start(f32[128,128]{1,0:T(8,128)S(1)} %bitcast.313), channel_id=1, source_target_pairs={{0,2},{1,3},{2,0},{3,1},{4,6},{5,7},{6,4},{7,5},{8,10},{9,11},{10,... | collective-permute-start | bytes 196616 | tf_op jit(solution)/shard_map/ppermute | solution.py:39
  33.4 7.6 %collective-permute-start.4 = (f32[128,128]{1,0:T(8,128)S(1)}, f32[128,128]{1,0:T(8,128)S(1)}, u32[]{:S(2)}, u32[]{:S(2)}) collective-permute-start(f32[128,128]{1,0:T(8,128)S(1)} %add.200), channel_id=1, source_target_pairs={{0,8},{4,12},{8,16},{12,20},{16,24},{20,28},{24,0},{28,4},{32,40},... | collective-permute-start | bytes 196616 | tf_op jit(solution)/shard_map/ppermute | solution.py:39
  35.3 8.0 %collective-permute-start.5 = (f32[128,128]{1,0:T(8,128)S(1)}, f32[128,128]{1,0:T(8,128)S(1)}, u32[]{:S(2)}, u32[]{:S(2)}) collective-permute-start(f32[128,128]{1,0:T(8,128)S(1)} %add.200), channel_id=1, source_target_pairs={{0,16},{4,20},{8,24},{12,28},{16,0},{20,4},{24,8},{28,12},{32,48},... | collective-permute-start | bytes 196616 | tf_op jit(solution)/shard_map/ppermute | solution.py:39
  44.5 8.3 %collective-permute-start.7 = (f32[128,128]{1,0:T(8,128)S(1)}, f32[128,128]{1,0:T(8,128)S(1)}, u32[]{:S(2)}, u32[]{:S(2)}) collective-permute-start(f32[128,128]{1,0:T(8,128)S(1)} %select_reduce_fusion.13), channel_id=1, source_target_pairs={{0,32},{4,36},{8,40},{12,44},{16,48},{20,52},{24,56},{28,60},{32,0... | collective-permute-start | bytes 196616 | tf_op jit(solution)/shard_map/ppermute | solution.py:28
  54.4 5.9 %collective-permute-start.9 = (f32[128,128]{1,0:T(8,128)S(1)}, f32[128,128]{1,0:T(8,128)S(1)}, u32[]{:S(2)}, u32[]{:S(2)}) collective-permute-start(f32[128,128]{1,0:T(8,128)S(1)} %add.203), channel_id=1, source_target_pairs={{0,128},{4,132},{8,136},{12,140},{16,144},{20,148},{24,152},{28,15... | collective-permute-start | bytes 196616 | tf_op jit(solution)/shard_map/ppermute | solution.py:39
  85.8 185.3 %all-gather.5.cloned.1.call-start = ((), (), s32[]{:S(2)}) async-start(), calls=%async_computation.3 | async-start | bytes 1310720 | tf_op jit(solution)/shard_map/all_gather | solution.py:118
  116.8 7.3 %collective-permute-start.11 = (bf16[128,3,256]{2,0,1:T(8,128)(2,1)S(1)}, bf16[128,3,256]{2,0,1:T(8,128)(2,1)S(1)}, u32[]{:S(2)}, u32[]{:S(2)}) collective-permute-start(bf16[128,3,256]{2,0,1:T(8,128)(2,1)S(1)} %get-tuple-element.27), channel_id=1, source_target_pairs={{0,4},{4,8},{8,12},{12,16},{16,20},{20,24},{24,28},{28,32},{32,36}... | collective-permute-start | bytes 589832 | tf_op jit(solution)/shard_map/ppermute | solution.py:17
  116.9 7.2 %collective-permute-start.12 = (bf16[128,3,256]{2,0,1:T(8,128)(2,1)S(1)}, bf16[128,3,256]{2,0,1:T(8,128)(2,1)S(1)}, u32[]{:S(2)}, u32[]{:S(2)}) collective-permute-start(bf16[128,3,256]{2,0,1:T(8,128)(2,1)S(1)} %get-tuple-element.28), channel_id=1, source_target_pairs={{4,0},{8,4},{12,8},{16,12},{20,16},{24,20},{28,24},{32,28},{36,32}... | collective-permute-start | bytes 589832 | tf_op jit(solution)/shard_map/ppermute | solution.py:19
  145.2 6.9 %collective-permute-start.13 = (f32[129,128]{1,0:T(8,128)S(1)}, f32[129,128]{1,0:T(8,128)S(1)}, u32[]{:S(2)}, u32[]{:S(2)}) collective-permute-start(f32[129,128]{1,0:T(8,128)S(1)} %get-tuple-element.34), channel_id=1, source_target_pairs={{0,1},{1,2},{2,3},{3,0},{4,5},{5,6},{6,7},{7,4},{8,9},{9,10},{10,1... | collective-permute-start | bytes 198152 | tf_op jit(solution)/shard_map/ppermute | solution.py:39
  145.6 6.5 %collective-permute-start.14 = (f32[129,128]{1,0:T(8,128)S(1)}, f32[129,128]{1,0:T(8,128)S(1)}, u32[]{:S(2)}, u32[]{:S(2)}) collective-permute-start(f32[129,128]{1,0:T(8,128)S(1)} %get-tuple-element.34), channel_id=1, source_target_pairs={{0,2},{1,3},{2,0},{3,1},{4,6},{5,7},{6,4},{7,5},{8,10},{9,11},{10,... | collective-permute-start | bytes 198152 | tf_op jit(solution)/shard_map/ppermute | solution.py:39
  154.7 7.0 %collective-permute-start.17 = (f32[129,128]{1,0:T(8,128)S(1)}, f32[129,128]{1,0:T(8,128)S(1)}, u32[]{:S(2)}, u32[]{:S(2)}) collective-permute-start(f32[129,128]{1,0:T(8,128)S(1)} %add.217), channel_id=1, source_target_pairs={{0,8},{4,12},{8,16},{12,20},{16,24},{20,28},{24,0},{28,4},{32,40},... | collective-permute-start | bytes 198152 | tf_op jit(solution)/shard_map/ppermute | solution.py:39
  154.9 9.3 %collective-permute-start.18 = (f32[129,128]{1,0:T(8,128)S(1)}, f32[129,128]{1,0:T(8,128)S(1)}, u32[]{:S(2)}, u32[]{:S(2)}) collective-permute-start(f32[129,128]{1,0:T(8,128)S(1)} %add.217), channel_id=1, source_target_pairs={{0,16},{4,20},{8,24},{12,28},{16,0},{20,4},{24,8},{28,12},{32,48},... | collective-permute-start | bytes 198152 | tf_op jit(solution)/shard_map/ppermute | solution.py:39
  159.0 5.6 %collective-permute-start.19 = (f32[129,128]{1,0:T(8,128)S(1)}, f32[129,128]{1,0:T(8,128)S(1)}, u32[]{:S(2)}, u32[]{:S(2)}) collective-permute-start(f32[129,128]{1,0:T(8,128)S(1)} %add.217), channel_id=1, source_target_pairs={{0,24},{4,28},{8,0},{12,4},{16,8},{20,12},{24,16},{28,20},{32,56},... | collective-permute-start | bytes 198152 | tf_op jit(solution)/shard_map/ppermute | solution.py:39
  165.2 9.0 %collective-permute-start.20 = (f32[129,128]{1,0:T(8,128)S(1)}, f32[129,128]{1,0:T(8,128)S(1)}, u32[]{:S(2)}, u32[]{:S(2)}) collective-permute-start(f32[129,128]{1,0:T(8,128)S(1)} %select_reduce_fusion.4), channel_id=1, source_target_pairs={{0,32},{4,36},{8,40},{12,44},{16,48},{20,52},{24,56},{28,60},{32,0... | collective-permute-start | bytes 198152 | tf_op jit(solution)/shard_map/ppermute | solution.py:28
  175.8 5.9 %collective-permute-start.22 = (f32[129,128]{1,0:T(8,128)S(1)}, f32[129,128]{1,0:T(8,128)S(1)}, u32[]{:S(2)}, u32[]{:S(2)}) collective-permute-start(f32[129,128]{1,0:T(8,128)S(1)} %add.218), channel_id=1, source_target_pairs={{0,128},{4,132},{8,136},{12,140},{16,144},{20,148},{24,152},{28,15... | collective-permute-start | bytes 198152 | tf_op jit(solution)/shard_map/ppermute | solution.py:39
  183.2 6.0 %collective-permute-start.24 = (f32[128,128]{1,0:T(8,128)S(1)}, f32[128,128]{1,0:T(8,128)S(1)}, u32[]{:S(2)}, u32[]{:S(2)}) collective-permute-start(f32[128,128]{1,0:T(8,128)S(1)} %fusion.155), channel_id=1, source_target_pairs={{0,1},{1,2},{2,3},{3,0},{4,5},{5,6},{6,7},{7,4},{8,9},{9,10},{10,1... | collective-permute-start | bytes 196616 | tf_op jit(solution)/shard_map/ppermute | solution.py:39
  185.2 5.8 %collective-permute-start.25 = (f32[128,128]{1,0:T(8,128)S(1)}, f32[128,128]{1,0:T(8,128)S(1)}, u32[]{:S(2)}, u32[]{:S(2)}) collective-permute-start(f32[128,128]{1,0:T(8,128)S(1)} %fusion.155), channel_id=1, source_target_pairs={{0,2},{1,3},{2,0},{3,1},{4,6},{5,7},{6,4},{7,5},{8,10},{9,11},{10,... | collective-permute-start | bytes 196616 | tf_op jit(solution)/shard_map/ppermute | solution.py:39
  194.3 6.9 %collective-permute-start.28 = (f32[128,128]{1,0:T(8,128)S(1)}, f32[128,128]{1,0:T(8,128)S(1)}, u32[]{:S(2)}, u32[]{:S(2)}) collective-permute-start(f32[128,128]{1,0:T(8,128)S(1)} %add.219), channel_id=1, source_target_pairs={{0,8},{4,12},{8,16},{12,20},{16,24},{20,28},{24,0},{28,4},{32,40},... | collective-permute-start | bytes 196616 | tf_op jit(solution)/shard_map/ppermute | solution.py:39
  195.8 7.4 %collective-permute-start.29 = (f32[128,128]{1,0:T(8,128)S(1)}, f32[128,128]{1,0:T(8,128)S(1)}, u32[]{:S(2)}, u32[]{:S(2)}) collective-permute-start(f32[128,128]{1,0:T(8,128)S(1)} %add.219), channel_id=1, source_target_pairs={{0,16},{4,20},{8,24},{12,28},{16,0},{20,4},{24,8},{28,12},{32,48},... | collective-permute-start | bytes 196616 | tf_op jit(solution)/shard_map/ppermute | solution.py:39
  197.4 5.9 %collective-permute-start.30 = (f32[128,128]{1,0:T(8,128)S(1)}, f32[128,128]{1,0:T(8,128)S(1)}, u32[]{:S(2)}, u32[]{:S(2)}) collective-permute-start(f32[128,128]{1,0:T(8,128)S(1)} %add.219), channel_id=1, source_target_pairs={{0,24},{4,28},{8,0},{12,4},{16,8},{20,12},{24,16},{28,20},{32,56},... | collective-permute-start | bytes 196616 | tf_op jit(solution)/shard_map/ppermute | solution.py:39
  203.9 9.0 %collective-permute-start.31 = (f32[128,128]{1,0:T(8,128)S(1)}, f32[128,128]{1,0:T(8,128)S(1)}, u32[]{:S(2)}, u32[]{:S(2)}) collective-permute-start(f32[128,128]{1,0:T(8,128)S(1)} %select_reduce_fusion.10), channel_id=1, source_target_pairs={{0,32},{4,36},{8,40},{12,44},{16,48},{20,52},{24,56},{28,60},{32,0... | collective-permute-start | bytes 196616 | tf_op jit(solution)/shard_map/ppermute | solution.py:28
  212.9 6.4 %collective-permute-start.32 = (f32[128,128]{1,0:T(8,128)S(1)}, f32[128,128]{1,0:T(8,128)S(1)}, u32[]{:S(2)}, u32[]{:S(2)}) collective-permute-start(f32[128,128]{1,0:T(8,128)S(1)} %add.220), channel_id=1, source_target_pairs={{0,64},{4,68},{8,72},{12,76},{16,80},{20,84},{24,88},{28,92},{32,9... | collective-permute-start | bytes 196616 | tf_op jit(solution)/shard_map/ppermute | solution.py:39
  214.6 5.8 %collective-permute-start.33 = (f32[128,128]{1,0:T(8,128)S(1)}, f32[128,128]{1,0:T(8,128)S(1)}, u32[]{:S(2)}, u32[]{:S(2)}) collective-permute-start(f32[128,128]{1,0:T(8,128)S(1)} %add.220), channel_id=1, source_target_pairs={{0,128},{4,132},{8,136},{12,140},{16,144},{20,148},{24,152},{28,15... | collective-permute-start | bytes 196616 | tf_op jit(solution)/shard_map/ppermute | solution.py:39
  272.7 7.3 %collective-permute-start.35 = (bf16[128,3,256]{2,0,1:T(8,128)(2,1)S(1)}, bf16[128,3,256]{2,0,1:T(8,128)(2,1)S(1)}, u32[]{:S(2)}, u32[]{:S(2)}) collective-permute-start(bf16[128,3,256]{2,0,1:T(8,128)(2,1)S(1)} %get-tuple-element.25), channel_id=1, source_target_pairs={{0,4},{4,8},{8,12},{12,16},{16,20},{20,24},{24,28},{28,32},{32,36}... | collective-permute-start | bytes 589832 | tf_op jit(solution)/shard_map/ppermute | solution.py:17
  272.8 7.2 %collective-permute-start.36 = (bf16[128,3,256]{2,0,1:T(8,128)(2,1)S(1)}, bf16[128,3,256]{2,0,1:T(8,128)(2,1)S(1)}, u32[]{:S(2)}, u32[]{:S(2)}) collective-permute-start(bf16[128,3,256]{2,0,1:T(8,128)(2,1)S(1)} %get-tuple-element.26), channel_id=1, source_target_pairs={{4,0},{8,4},{12,8},{16,12},{20,16},{24,20},{28,24},{32,28},{36,32}... | collective-permute-start | bytes 589832 | tf_op jit(solution)/shard_map/ppermute | solution.py:19
  301.2 9.7 %collective-permute-start.37 = (f32[257,128]{1,0:T(8,128)S(1)}, f32[257,128]{1,0:T(8,128)S(1)}, u32[]{:S(2)}, u32[]{:S(2)}) collective-permute-start(f32[257,128]{1,0:T(8,128)S(1)} %get-tuple-element.32), channel_id=1, source_target_pairs={{0,1},{1,2},{2,3},{3,0},{4,5},{5,6},{6,7},{7,4},{8,9},{9,10},{10,1... | collective-permute-start | bytes 394760 | tf_op jit(solution)/shard_map/ppermute | solution.py:39
  301.6 9.3 %collective-permute-start.38 = (f32[257,128]{1,0:T(8,128)S(1)}, f32[257,128]{1,0:T(8,128)S(1)}, u32[]{:S(2)}, u32[]{:S(2)}) collective-permute-start(f32[257,128]{1,0:T(8,128)S(1)} %get-tuple-element.32), channel_id=1, source_target_pairs={{0,2},{1,3},{2,0},{3,1},{4,6},{5,7},{6,4},{7,5},{8,10},{9,11},{10,... | collective-permute-start | bytes 394760 | tf_op jit(solution)/shard_map/ppermute | solution.py:39
  304.3 7.2 %collective-permute-start.39 = (f32[257,128]{1,0:T(8,128)S(1)}, f32[257,128]{1,0:T(8,128)S(1)}, u32[]{:S(2)}, u32[]{:S(2)}) collective-permute-start(f32[257,128]{1,0:T(8,128)S(1)} %get-tuple-element.32), channel_id=1, source_target_pairs={{0,3},{1,0},{2,1},{3,2},{4,7},{5,4},{6,5},{7,6},{8,11},{9,8},{10,9... | collective-permute-start | bytes 394760 | tf_op jit(solution)/shard_map/ppermute | solution.py:39
  313.7 8.4 %collective-permute-start.41 = (f32[257,128]{1,0:T(8,128)S(1)}, f32[257,128]{1,0:T(8,128)S(1)}, u32[]{:S(2)}, u32[]{:S(2)}) collective-permute-start(f32[257,128]{1,0:T(8,128)S(1)} %add.229), channel_id=1, source_target_pairs={{0,8},{4,12},{8,16},{12,20},{16,24},{20,28},{24,0},{28,4},{32,40},... | collective-permute-start | bytes 394760 | tf_op jit(solution)/shard_map/ppermute | solution.py:39
  313.9 13.1 %collective-permute-start.42 = (f32[257,128]{1,0:T(8,128)S(1)}, f32[257,128]{1,0:T(8,128)S(1)}, u32[]{:S(2)}, u32[]{:S(2)}) collective-permute-start(f32[257,128]{1,0:T(8,128)S(1)} %add.229), channel_id=1, source_target_pairs={{0,16},{4,20},{8,24},{12,28},{16,0},{20,4},{24,8},{28,12},{32,48},... | collective-permute-start | bytes 394760 | tf_op jit(solution)/shard_map/ppermute | solution.py:39
  316.6 10.5 %collective-permute-start.43 = (f32[257,128]{1,0:T(8,128)S(1)}, f32[257,128]{1,0:T(8,128)S(1)}, u32[]{:S(2)}, u32[]{:S(2)}) collective-permute-start(f32[257,128]{1,0:T(8,128)S(1)} %add.229), channel_id=1, source_target_pairs={{0,24},{4,28},{8,0},{12,4},{16,8},{20,12},{24,16},{28,20},{32,56},... | collective-permute-start | bytes 394760 | tf_op jit(solution)/shard_map/ppermute | solution.py:39
  327.8 9.1 %collective-permute-start.44 = (f32[257,128]{1,0:T(8,128)S(1)}, f32[257,128]{1,0:T(8,128)S(1)}, u32[]{:S(2)}, u32[]{:S(2)}) collective-permute-start(f32[257,128]{1,0:T(8,128)S(1)} %select_reduce_fusion.1), channel_id=1, source_target_pairs={{0,32},{4,36},{8,40},{12,44},{16,48},{20,52},{24,56},{28,60},{32,0... | collective-permute-start | bytes 394760 | tf_op jit(solution)/shard_map/ppermute | solution.py:28
  338.5 6.6 %collective-permute-start.46 = (f32[257,128]{1,0:T(8,128)S(1)}, f32[257,128]{1,0:T(8,128)S(1)}, u32[]{:S(2)}, u32[]{:S(2)}) collective-permute-start(f32[257,128]{1,0:T(8,128)S(1)} %add.230), channel_id=1, source_target_pairs={{0,128},{4,132},{8,136},{12,140},{16,144},{20,148},{24,152},{28,15... | collective-permute-start | bytes 394760 | tf_op jit(solution)/shard_map/ppermute | solution.py:39
  339.6 6.8 %collective-permute-start.47 = (f32[257,128]{1,0:T(8,128)S(1)}, f32[257,128]{1,0:T(8,128)S(1)}, u32[]{:S(2)}, u32[]{:S(2)}) collective-permute-start(f32[257,128]{1,0:T(8,128)S(1)} %add.230), channel_id=1, source_target_pairs={{0,192},{4,196},{8,200},{12,204},{16,208},{20,212},{24,216},{28,22... | collective-permute-start | bytes 394760 | tf_op jit(solution)/shard_map/ppermute | solution.py:39
  349.6 5.8 %collective-permute-start.49 = (f32[128,128]{1,0:T(8,128)S(1)}, f32[128,128]{1,0:T(8,128)S(1)}, u32[]{:S(2)}, u32[]{:S(2)}) collective-permute-start(f32[128,128]{1,0:T(8,128)S(1)} %fusion.156), channel_id=1, source_target_pairs={{0,2},{1,3},{2,0},{3,1},{4,6},{5,7},{6,4},{7,5},{8,10},{9,11},{10,... | collective-permute-start | bytes 196616 | tf_op jit(solution)/shard_map/ppermute | solution.py:39
  358.6 9.0 %collective-permute-start.52 = (f32[128,128]{1,0:T(8,128)S(1)}, f32[128,128]{1,0:T(8,128)S(1)}, u32[]{:S(2)}, u32[]{:S(2)}) collective-permute-start(f32[128,128]{1,0:T(8,128)S(1)} %add.231), channel_id=1, source_target_pairs={{0,8},{4,12},{8,16},{12,20},{16,24},{20,28},{24,0},{28,4},{32,40},... | collective-permute-start | bytes 196616 | tf_op jit(solution)/shard_map/ppermute | solution.py:39
  365.1 6.1 %collective-permute-start.53 = (f32[128,128]{1,0:T(8,128)S(1)}, f32[128,128]{1,0:T(8,128)S(1)}, u32[]{:S(2)}, u32[]{:S(2)}) collective-permute-start(f32[128,128]{1,0:T(8,128)S(1)} %add.231), channel_id=1, source_target_pairs={{0,16},{4,20},{8,24},{12,28},{16,0},{20,4},{24,8},{28,12},{32,48},... | collective-permute-start | bytes 196616 | tf_op jit(solution)/shard_map/ppermute | solution.py:39
  365.1 6.1 %collective-permute-start.54 = (f32[128,128]{1,0:T(8,128)S(1)}, f32[128,128]{1,0:T(8,128)S(1)}, u32[]{:S(2)}, u32[]{:S(2)}) collective-permute-start(f32[128,128]{1,0:T(8,128)S(1)} %add.231), channel_id=1, source_target_pairs={{0,24},{4,28},{8,0},{12,4},{16,8},{20,12},{24,16},{28,20},{32,56},... | collective-permute-start | bytes 196616 | tf_op jit(solution)/shard_map/ppermute | solution.py:39
  371.9 8.3 %collective-permute-start.55 = (f32[128,128]{1,0:T(8,128)S(1)}, f32[128,128]{1,0:T(8,128)S(1)}, u32[]{:S(2)}, u32[]{:S(2)}) collective-permute-start(f32[128,128]{1,0:T(8,128)S(1)} %select_reduce_fusion.7), channel_id=1, source_target_pairs={{0,32},{4,36},{8,40},{12,44},{16,48},{20,52},{24,56},{28,60},{32,0... | collective-permute-start | bytes 196616 | tf_op jit(solution)/shard_map/ppermute | solution.py:28
  381.2 5.8 %collective-permute-start.57 = (f32[128,128]{1,0:T(8,128)S(1)}, f32[128,128]{1,0:T(8,128)S(1)}, u32[]{:S(2)}, u32[]{:S(2)}) collective-permute-start(f32[128,128]{1,0:T(8,128)S(1)} %add.232), channel_id=1, source_target_pairs={{0,128},{4,132},{8,136},{12,140},{16,144},{20,148},{24,152},{28,15... | collective-permute-start | bytes 196616 | tf_op jit(solution)/shard_map/ppermute | solution.py:39
  428.3 7.5 %collective-permute-start.66 = (f32[128]{0:T(128)S(1)}, f32[128]{0:T(128)S(1)}, u32[]{:S(2)}, u32[]{:S(2)}) collective-permute-start(f32[128]{0:T(128)S(1)} %select_reduce_fusion.17), channel_id=1, source_target_pairs={{0,32},{4,36},{8,40},{12,44},{16,48},{20,52},{24,56},{28,60},{32,0... | collective-permute-start | bytes 1544 | tf_op jit(solution)/shard_map/ppermute | solution.py:28
  435.8 11.1 %collective-permute-start.67 = (f32[128]{0:T(128)S(1)}, f32[128]{0:T(128)S(1)}, u32[]{:S(2)}, u32[]{:S(2)}) collective-permute-start(f32[128]{0:T(128)S(1)} %add.234), channel_id=1, source_target_pairs={{0,64},{4,68},{8,72},{12,76},{16,80},{20,84},{24,88},{28,92},{32,9... | collective-permute-start | bytes 1544 | tf_op jit(solution)/shard_map/ppermute | solution.py:39
  436.7 10.1 %collective-permute-start.68 = (f32[128]{0:T(128)S(1)}, f32[128]{0:T(128)S(1)}, u32[]{:S(2)}, u32[]{:S(2)}) collective-permute-start(f32[128]{0:T(128)S(1)} %add.234), channel_id=1, source_target_pairs={{0,128},{4,132},{8,136},{12,140},{16,144},{20,148},{24,152},{28,15... | collective-permute-start | bytes 1544 | tf_op jit(solution)/shard_map/ppermute | solution.py:39
  439.5 7.4 %collective-permute-start.69 = (f32[128]{0:T(128)S(1)}, f32[128]{0:T(128)S(1)}, u32[]{:S(2)}, u32[]{:S(2)}) collective-permute-start(f32[128]{0:T(128)S(1)} %add.234), channel_id=1, source_target_pairs={{0,192},{4,196},{8,200},{12,204},{16,208},{20,212},{24,216},{28,22... | collective-permute-start | bytes 1544 | tf_op jit(solution)/shard_map/ppermute | solution.py:39
  443.0 10.6 %all-to-all-start.1 = ((bf16[4,2,16384]{2,1,0:T(2,128)(2,1)}), bf16[4,2,16384]{2,1,0:T(2,128)(2,1)S(1)}, u32[]{:S(2)}, u32[]{:S(2)}) async-start(bf16[4,2,16384]{2,1,0:T(2,128)(2,1)} %reshape.450), calls=%async_computation.1 | async-start | bytes 524288 | tf_op jit(solution)/shard_map/all_to_all | solution.py:143
  (39 other events, 208.9 us)
Sparse Core Ops, SparseCore 0:
  85.9 29.1 all-gather.2
  246.9 24.1 all-gather.4
where the time goes:
time: 471 us; the launch traced here: 462 us
  waiting for transfers between devices  166 us (35%)
  starting transfers between devices  137 us (29%)
  other arithmetic  72.8 us (15%)
  local copies, waits for them, and re-layouts  50.1 us (11%)
  matrix products  21.2 us (5%)
  between operations  15.3 us (3%)
    ppermute x54, starting transfers between devices, group_step(): vals.append(lax.ppermute(x, axis, perm))  92.1 us
    ppermute x54, waiting for transfers between devices, group_step(): vals.append(lax.ppermute(x, axis, perm))  65.2 us
    all_gather x2, waiting for transfers between devices, local(): gathered = lax.all_gather(basis_cube, 'cols', axis=2, tiled=True)  53.5 us
    another operation x9, other arithmetic, orthonormal(): lower = jnp.linalg.cholesky(gram)  37.2 us
    another operation x6, other arithmetic, orthonormal(): jax.scipy.linalg.solve_triangular(lower, identity, lower=True)  31.4 us
    ppermute x12, waiting for transfers between devices, pair_step(): return x + lax.ppermute(x, axis, perm)  30.6 us
    ppermute x12, starting transfers between devices, pair_step(): return x + lax.ppermute(x, axis, perm)  28.4 us
    gather x16, local copies, waits for them, and re-layouts, fold_slots(): picked = jnp.take(piece, local_index[:, slot], axis=1)  23.6 us
  transfers between devices with their start and end apart: 74, of which 57 were waited for; matrix products, arithmetic and copies ran while one was open for 1% of the time, Pallas kernels for 0%

commit v1 on v0

--- a/solution.py
+++ b/solution.py
@@ -115,7 +115,9 @@
         image_count = basis_now.shape[0]
         basis_cube = basis_now.reshape(image_count, tiles_here, voxels_here)
         empty = jnp.zeros((image_count, tiles_here, voxels_here), jnp.float32)
-        gathered = lax.all_gather(basis_cube, "cols", axis=2, tiled=True)
+        gathered = jnp.concatenate(
+            lax.all_to_all(jnp.stack([basis_cube] * lax.axis_size("cols")), "cols", 0, 0), axis=2
+        )
         padded = with_halo(gathered, (("tiles", 1),), REACH)
         total = fold_slots(empty, padded, cov_blocks, local_index)
         image = (total * mask_values[None]).astype(jnp.bfloat16).reshape(image_count, -1)

time: 471 us -> 436 us (0.926)
  the two profiles are of different devices: /device:TPU:8 before, /device:TPU:32 now
where the time goes in v1:
time: 436 us; the launch traced here: 427 us
  waiting for transfers between devices  152 us (35%)
  starting transfers between devices  113 us (26%)
  other arithmetic  72.8 us (17%)
  local copies, waits for them, and re-layouts  49.8 us (11%)
  matrix products  21.2 us (5%)
  blocking collectives  16.3 us (4%)
    ppermute x54, waiting for transfers between devices, group_step(): vals.append(lax.ppermute(x, axis, perm))  82.2 us
    ppermute x54, starting transfers between devices, group_step(): vals.append(lax.ppermute(x, axis, perm))  74.9 us
    ppermute x12, waiting for transfers between devices, pair_step(): return x + lax.ppermute(x, axis, perm)  41.9 us
    another operation x9, other arithmetic, orthonormal(): lower = jnp.linalg.cholesky(gram)  37.2 us
    another operation x6, other arithmetic, orthonormal(): jax.scipy.linalg.solve_triangular(lower, identity, lower=True)  31.4 us
    gather x16, local copies, waits for them, and re-layouts, fold_slots(): picked = jnp.take(piece, local_index[:, slot], axis=1)  23.6 us
    ppermute x12, starting transfers between devices, pair_step(): return x + lax.ppermute(x, axis, perm)  22.5 us
    dot_general x16, matrix products, fold_slots(): jnp.einsum('iuv,biv->biu', blocks, picked, preferred_element_type=jnp.flo...  17.4 us
  transfers between devices with their start and end apart: 73, of which 61 were waited for; matrix products, arithmetic and copies ran while one was open for 1% of the time, Pallas kernels for 0%

profile of v1, /device:TPU:32, one launch (start us, length us, event | category | flops | bytes accessed | tf_op | source)
XLA Modules:
  0.0 427.3 jit_solution(5243140925792828616)
XLA Ops:
  4.7 4.3 %all-to-all-start = ((bf16[4,2,16384]{2,1,0:T(2,128)(2,1)}), bf16[4,2,16384]{2,1,0:T(2,128)(2,1)S(1)}, u32[]{:S(2)}, u32[]{:S(2)}) async-start(bf16[4,2,16384]{2,1,0:T(2,128)(2,1)} %reshape.460), calls=%async_computation | async-start | bytes 524288 | tf_op jit(solution)/shard_map/all_to_all | solution.py:104
  10.5 5.1 %all-to-all-done = bf16[4,2,16384]{2,1,0:T(2,128)(2,1)S(1)} async-done(((bf16[4,2,16384]{2,1,0:T(2,128)(2,1)}), bf16[4,2,16384]{2,1,0:T(2,128)(2,1)S(1)}, u32[]{:S(2)}, u32[]{:S(2)}) %all-to-all-start) | async-done | bytes 262176 | tf_op jit(solution)/shard_map/all_to_all | solution.py:104
  32.2 2.7 collective-permute-done.5
  37.5 6.0 %collective-permute-start.7 = (f32[128,128]{1,0:T(8,128)S(1)}, f32[128,128]{1,0:T(8,128)S(1)}, u32[]{:S(2)}, u32[]{:S(2)}) collective-permute-start(f32[128,128]{1,0:T(8,128)S(1)} %select_reduce_fusion.13), channel_id=1, source_target_pairs={{0,32},{4,36},{8,40},{12,44},{16,48},{20,52},{24,56},{28,60},{32,0... | collective-permute-start | bytes 196616 | tf_op jit(solution)/shard_map/ppermute | solution.py:28
  43.5 3.6 collective-permute-done.7
  48.8 2.9 collective-permute-start.9
  56.9 11.7 %cholesky.59 = f32[128,128]{1,0:T(8,128)S(1)} custom-call(f32[128,128]{1,0:T(8,128)S(1)} %fusion.122), custom_call_target="Cholesky" | custom-call | tf_op jit(solution)/shard_map/jit(cholesky)/cholesky | solution.py:75
  70.0 9.8 %custom-call.7 = f32[1,128,128]{1,2,0:T(8,128)S(1)} custom-call(f32[1,128,128]{2,1,0:T(8,128)S(1)} %fusion.114), custom_call_target="InvertDiagBlocksLowerTriangular" | custom-call | tf_op jit(solution)/shard_map/jit(_solve_triangular)/triangular_solve | solution.py:77
  81.8 3.7 all-to-all-start.1
  85.6 11.4 %all-to-all-done.1 = bf16[4,128,16,64]{1,3,2,0:T(8,128)(2,1)S(1)} async-done(((bf16[4,128,16,64]{1,3,2,0:T(8,128)(2,1)}), bf16[4,128,16,64]{1,3,2,0:T(8,128)(2,1)S(1)}, u32[]{:S(2)}, u32[]{:S(2)}) %all-to-all-start.1) | async-done | bytes 1048608 | tf_op jit(solution)/shard_map/all_to_all | solution.py:119
  101.7 3.1 collective-permute-done.11
  129.4 3.5 collective-permute-done.13
  136.3 4.9 %collective-permute-start.18 = (f32[129,128]{1,0:T(8,128)S(1)}, f32[129,128]{1,0:T(8,128)S(1)}, u32[]{:S(2)}, u32[]{:S(2)}) collective-permute-start(f32[129,128]{1,0:T(8,128)S(1)} %add.217), channel_id=1, source_target_pairs={{0,16},{4,20},{8,24},{12,28},{16,0},{20,4},{24,8},{28,12},{32,48},... | collective-permute-start | bytes 198152 | tf_op jit(solution)/shard_map/ppermute | solution.py:39
  141.9 3.8 collective-permute-done.18
  148.1 4.6 %collective-permute-start.20 = (f32[129,128]{1,0:T(8,128)S(1)}, f32[129,128]{1,0:T(8,128)S(1)}, u32[]{:S(2)}, u32[]{:S(2)}) collective-permute-start(f32[129,128]{1,0:T(8,128)S(1)} %select_reduce_fusion.4), channel_id=1, source_target_pairs={{0,32},{4,36},{8,40},{12,44},{16,48},{20,52},{24,56},{28,60},{32,0... | collective-permute-start | bytes 198152 | tf_op jit(solution)/shard_map/ppermute | solution.py:28
  152.6 5.0 %collective-permute-done.20 = f32[129,128]{1,0:T(8,128)S(1)} collective-permute-done((f32[129,128]{1,0:T(8,128)S(1)}, f32[129,128]{1,0:T(8,128)S(1)}, u32[]{:S(2)}, u32[]{:S(2)}) %collective-permute-start.20) | collective-permute-done | bytes 66080 | tf_op jit(solution)/shard_map/ppermute | solution.py:28
  157.8 3.8 collective-permute-start.22
  167.5 3.8 collective-permute-start.25
  177.8 2.4 collective-permute-start.29
  187.2 4.0 collective-permute-start.31
  191.3 5.4 %collective-permute-done.31 = f32[128,128]{1,0:T(8,128)S(1)} collective-permute-done((f32[128,128]{1,0:T(8,128)S(1)}, f32[128,128]{1,0:T(8,128)S(1)}, u32[]{:S(2)}, u32[]{:S(2)}) %collective-permute-start.31) | collective-permute-done | bytes 65568 | tf_op jit(solution)/shard_map/ppermute | solution.py:28
  197.1 2.9 collective-permute-start.33
  205.2 11.7 %cholesky.70 = f32[128,128]{1,0:T(8,128)S(1)} custom-call(f32[128,128]{1,0:T(8,128)S(1)} %fusion.120), custom_call_target="Cholesky" | custom-call | tf_op jit(solution)/shard_map/jit(cholesky)/cholesky | solution.py:75
  218.2 9.8 %custom-call.8 = f32[1,128,128]{1,2,0:T(8,128)S(1)} custom-call(f32[1,128,128]{2,1,0:T(8,128)S(1)} %fusion.115), custom_call_target="InvertDiagBlocksLowerTriangular" | custom-call | tf_op jit(solution)/shard_map/jit(_solve_triangular)/triangular_solve | solution.py:77
  229.1 16.3 %all_to_all.37 = bf16[4,128,16,64]{1,3,2,0:T(8,128)(2,1)S(1)} all-to-all(bf16[4,128,16,64]{1,3,2,0:T(8,128)(2,1)S(1)} %stack.328), channel_id=1, replica_groups=mesh['tiles'=64,'cols'=4] {'cols'}, dimensions={0} | all-to-all | bytes 2097152 | tf_op jit(solution)/shard_map/all_to_all | solution.py:119
  248.1 3.2 collective-permute-done.35
  275.4 2.8 collective-permute-done.39
  278.2 3.2 collective-permute-done.37
  283.7 6.3 %collective-permute-start.42 = (f32[257,128]{1,0:T(8,128)S(1)}, f32[257,128]{1,0:T(8,128)S(1)}, u32[]{:S(2)}, u32[]{:S(2)}) collective-permute-start(f32[257,128]{1,0:T(8,128)S(1)} %add.229), channel_id=1, source_target_pairs={{0,16},{4,20},{8,24},{12,28},{16,0},{20,4},{24,8},{28,12},{32,48},... | collective-permute-start | bytes 394760 | tf_op jit(solution)/shard_map/ppermute | solution.py:39
  292.1 6.6 %collective-permute-done.42 = f32[257,128]{1,0:T(8,128)S(1)} collective-permute-done((f32[257,128]{1,0:T(8,128)S(1)}, f32[257,128]{1,0:T(8,128)S(1)}, u32[]{:S(2)}, u32[]{:S(2)}) %collective-permute-start.42) | collective-permute-done | bytes 131616 | tf_op jit(solution)/shard_map/ppermute | solution.py:39
  298.7 2.9 collective-permute-done.43
  302.3 2.5 collective-permute-start.44
  304.8 9.2 %collective-permute-done.44 = f32[257,128]{1,0:T(8,128)S(1)} collective-permute-done((f32[257,128]{1,0:T(8,128)S(1)}, f32[257,128]{1,0:T(8,128)S(1)}, u32[]{:S(2)}, u32[]{:S(2)}) %collective-permute-start.44) | collective-permute-done | bytes 131616 | tf_op jit(solution)/shard_map/ppermute | solution.py:28
  314.1 2.5 collective-permute-start.46
  317.9 5.6 %collective-permute-done.45 = f32[257,128]{1,0:T(8,128)S(1)} collective-permute-done((f32[257,128]{1,0:T(8,128)S(1)}, f32[257,128]{1,0:T(8,128)S(1)}, u32[]{:S(2)}, u32[]{:S(2)}) %collective-permute-start.45) | collective-permute-done | bytes 131616 | tf_op jit(solution)/shard_map/ppermute | solution.py:39
  329.4 2.4 collective-permute-done.48
  336.9 2.8 collective-permute-done.52
  343.5 2.5 collective-permute-start.55
  346.0 6.2 %collective-permute-done.55 = f32[128,128]{1,0:T(8,128)S(1)} collective-permute-done((f32[128,128]{1,0:T(8,128)S(1)}, f32[128,128]{1,0:T(8,128)S(1)}, u32[]{:S(2)}, u32[]{:S(2)}) %collective-permute-start.55) | collective-permute-done | bytes 65568 | tf_op jit(solution)/shard_map/ppermute | solution.py:28
  353.1 3.5 collective-permute-start.57
  361.8 11.7 %cholesky.81 = f32[128,128]{1,0:T(8,128)S(1)} custom-call(f32[128,128]{1,0:T(8,128)S(1)} %fusion.118), custom_call_target="Cholesky" | custom-call | tf_op jit(solution)/shard_map/jit(cholesky)/cholesky | solution.py:75
  374.9 9.8 %custom-call.9 = f32[1,128,128]{1,2,0:T(8,128)S(1)} custom-call(f32[1,128,128]{2,1,0:T(8,128)S(1)} %fusion.116), custom_call_target="InvertDiagBlocksLowerTriangular" | custom-call | tf_op jit(solution)/shard_map/jit(_solve_triangular)/triangular_solve | solution.py:77
  386.5 2.9 collective-permute-start.60
  394.8 2.7 collective-permute-start.64
  404.2 5.1 %collective-permute-done.66 = f32[128]{0:T(128)S(1)} collective-permute-done((f32[128]{0:T(128)S(1)}, f32[128]{0:T(128)S(1)}, u32[]{:S(2)}, u32[]{:S(2)}) %collective-permute-start.66) | collective-permute-done | bytes 544 | tf_op jit(solution)/shard_map/ppermute | solution.py:28
  409.5 2.7 collective-permute-start.68
  415.2 3.4 all-to-all-start.3
  419.9 5.4 %all-to-all-done.3 = bf16[4,2,16384]{2,1,0:T(2,128)(2,1)S(1)} async-done(((bf16[4,2,16384]{2,1,0:T(2,128)(2,1)}), bf16[4,2,16384]{2,1,0:T(2,128)(2,1)S(1)}, u32[]{:S(2)}, u32[]{:S(2)}) %all-to-all-start.3) | async-done | bytes 262176 | tf_op jit(solution)/shard_map/all_to_all | solution.py:145
  (308 shorter events, 172.9 us)
Async XLA Ops:
  4.7 11.0 %all-to-all-start = ((bf16[4,2,16384]{2,1,0:T(2,128)(2,1)}), bf16[4,2,16384]{2,1,0:T(2,128)(2,1)S(1)}, u32[]{:S(2)}, u32[]{:S(2)}) async-start(bf16[4,2,16384]{2,1,0:T(2,128)(2,1)} %reshape.460), calls=%async_computation | async-start | bytes 524288 | tf_op jit(solution)/shard_map/all_to_all | solution.py:104
  17.6 5.6 %collective-permute-start = (f32[128,128]{1,0:T(8,128)S(1)}, f32[128,128]{1,0:T(8,128)S(1)}, u32[]{:S(2)}, u32[]{:S(2)}) collective-permute-start(f32[128,128]{1,0:T(8,128)S(1)} %bitcast.320), channel_id=1, source_target_pairs={{0,1},{1,2},{2,3},{3,0},{4,5},{5,6},{6,7},{7,4},{8,9},{9,10},{10,1... | collective-permute-start | bytes 196616 | tf_op jit(solution)/shard_map/ppermute | solution.py:39
  18.3 5.8 %collective-permute-start.1 = (f32[128,128]{1,0:T(8,128)S(1)}, f32[128,128]{1,0:T(8,128)S(1)}, u32[]{:S(2)}, u32[]{:S(2)}) collective-permute-start(f32[128,128]{1,0:T(8,128)S(1)} %bitcast.321), channel_id=1, source_target_pairs={{0,2},{1,3},{2,0},{3,1},{4,6},{5,7},{6,4},{7,5},{8,10},{9,11},{10,... | collective-permute-start | bytes 196616 | tf_op jit(solution)/shard_map/ppermute | solution.py:39
  26.8 5.4 %collective-permute-start.4 = (f32[128,128]{1,0:T(8,128)S(1)}, f32[128,128]{1,0:T(8,128)S(1)}, u32[]{:S(2)}, u32[]{:S(2)}) collective-permute-start(f32[128,128]{1,0:T(8,128)S(1)} %add.200), channel_id=1, source_target_pairs={{0,8},{4,12},{8,16},{12,20},{16,24},{20,28},{24,0},{28,4},{32,40},... | collective-permute-start | bytes 196616 | tf_op jit(solution)/shard_map/ppermute | solution.py:39
  28.8 6.1 %collective-permute-start.5 = (f32[128,128]{1,0:T(8,128)S(1)}, f32[128,128]{1,0:T(8,128)S(1)}, u32[]{:S(2)}, u32[]{:S(2)}) collective-permute-start(f32[128,128]{1,0:T(8,128)S(1)} %add.200), channel_id=1, source_target_pairs={{0,16},{4,20},{8,24},{12,28},{16,0},{20,4},{24,8},{28,12},{32,48},... | collective-permute-start | bytes 196616 | tf_op jit(solution)/shard_map/ppermute | solution.py:39
  30.2 6.5 %collective-permute-start.6 = (f32[128,128]{1,0:T(8,128)S(1)}, f32[128,128]{1,0:T(8,128)S(1)}, u32[]{:S(2)}, u32[]{:S(2)}) collective-permute-start(f32[128,128]{1,0:T(8,128)S(1)} %add.200), channel_id=1, source_target_pairs={{0,24},{4,28},{8,0},{12,4},{16,8},{20,12},{24,16},{28,20},{32,56},... | collective-permute-start | bytes 196616 | tf_op jit(solution)/shard_map/ppermute | solution.py:39
  37.5 9.6 %collective-permute-start.7 = (f32[128,128]{1,0:T(8,128)S(1)}, f32[128,128]{1,0:T(8,128)S(1)}, u32[]{:S(2)}, u32[]{:S(2)}) collective-permute-start(f32[128,128]{1,0:T(8,128)S(1)} %select_reduce_fusion.13), channel_id=1, source_target_pairs={{0,32},{4,36},{8,40},{12,44},{16,48},{20,52},{24,56},{28,60},{32,0... | collective-permute-start | bytes 196616 | tf_op jit(solution)/shard_map/ppermute | solution.py:28
  47.1 6.4 %collective-permute-start.8 = (f32[128,128]{1,0:T(8,128)S(1)}, f32[128,128]{1,0:T(8,128)S(1)}, u32[]{:S(2)}, u32[]{:S(2)}) collective-permute-start(f32[128,128]{1,0:T(8,128)S(1)} %add.203), channel_id=1, source_target_pairs={{0,64},{4,68},{8,72},{12,76},{16,80},{20,84},{24,88},{28,92},{32,9... | collective-permute-start | bytes 196616 | tf_op jit(solution)/shard_map/ppermute | solution.py:39
  48.8 5.8 %collective-permute-start.9 = (f32[128,128]{1,0:T(8,128)S(1)}, f32[128,128]{1,0:T(8,128)S(1)}, u32[]{:S(2)}, u32[]{:S(2)}) collective-permute-start(f32[128,128]{1,0:T(8,128)S(1)} %add.203), channel_id=1, source_target_pairs={{0,128},{4,132},{8,136},{12,140},{16,144},{20,148},{24,152},{28,15... | collective-permute-start | bytes 196616 | tf_op jit(solution)/shard_map/ppermute | solution.py:39
  81.8 15.2 %all-to-all-start.1 = ((bf16[4,128,16,64]{1,3,2,0:T(8,128)(2,1)}), bf16[4,128,16,64]{1,3,2,0:T(8,128)(2,1)S(1)}, u32[]{:S(2)}, u32[]{:S(2)}) async-start(bf16[4,128,16,64]{1,3,2,0:T(8,128)(2,1)} %stack.297), calls=%async_computation.1 | async-start | bytes 2097152 | tf_op jit(solution)/shard_map/all_to_all | solution.py:119
  99.7 5.2 %collective-permute-start.11 = (bf16[128,3,256]{2,0,1:T(8,128)(2,1)S(1)}, bf16[128,3,256]{2,0,1:T(8,128)(2,1)S(1)}, u32[]{:S(2)}, u32[]{:S(2)}) collective-permute-start(bf16[128,3,256]{2,0,1:T(8,128)(2,1)S(1)} %get-tuple-element.27), channel_id=1, source_target_pairs={{0,4},{4,8},{8,12},{12,16},{16,20},{20,24},{24,28},{28,32},{32,36}... | collective-permute-start | bytes 589832 | tf_op jit(solution)/shard_map/ppermute | solution.py:17
  126.0 6.9 %collective-permute-start.13 = (f32[129,128]{1,0:T(8,128)S(1)}, f32[129,128]{1,0:T(8,128)S(1)}, u32[]{:S(2)}, u32[]{:S(2)}) collective-permute-start(f32[129,128]{1,0:T(8,128)S(1)} %get-tuple-element.34), channel_id=1, source_target_pairs={{0,1},{1,2},{2,3},{3,0},{4,5},{5,6},{6,7},{7,4},{8,9},{9,10},{10,1... | collective-permute-start | bytes 198152 | tf_op jit(solution)/shard_map/ppermute | solution.py:39
  126.6 6.3 %collective-permute-start.14 = (f32[129,128]{1,0:T(8,128)S(1)}, f32[129,128]{1,0:T(8,128)S(1)}, u32[]{:S(2)}, u32[]{:S(2)}) collective-permute-start(f32[129,128]{1,0:T(8,128)S(1)} %get-tuple-element.34), channel_id=1, source_target_pairs={{0,2},{1,3},{2,0},{3,1},{4,6},{5,7},{6,4},{7,5},{8,10},{9,11},{10,... | collective-permute-start | bytes 198152 | tf_op jit(solution)/shard_map/ppermute | solution.py:39
  135.5 6.4 %collective-permute-start.17 = (f32[129,128]{1,0:T(8,128)S(1)}, f32[129,128]{1,0:T(8,128)S(1)}, u32[]{:S(2)}, u32[]{:S(2)}) collective-permute-start(f32[129,128]{1,0:T(8,128)S(1)} %add.217), channel_id=1, source_target_pairs={{0,8},{4,12},{8,16},{12,20},{16,24},{20,28},{24,0},{28,4},{32,40},... | collective-permute-start | bytes 198152 | tf_op jit(solution)/shard_map/ppermute | solution.py:39
  136.3 9.4 %collective-permute-start.18 = (f32[129,128]{1,0:T(8,128)S(1)}, f32[129,128]{1,0:T(8,128)S(1)}, u32[]{:S(2)}, u32[]{:S(2)}) collective-permute-start(f32[129,128]{1,0:T(8,128)S(1)} %add.217), channel_id=1, source_target_pairs={{0,16},{4,20},{8,24},{12,28},{16,0},{20,4},{24,8},{28,12},{32,48},... | collective-permute-start | bytes 198152 | tf_op jit(solution)/shard_map/ppermute | solution.py:39
  141.2 6.2 %collective-permute-start.19 = (f32[129,128]{1,0:T(8,128)S(1)}, f32[129,128]{1,0:T(8,128)S(1)}, u32[]{:S(2)}, u32[]{:S(2)}) collective-permute-start(f32[129,128]{1,0:T(8,128)S(1)} %add.217), channel_id=1, source_target_pairs={{0,24},{4,28},{8,0},{12,4},{16,8},{20,12},{24,16},{28,20},{32,56},... | collective-permute-start | bytes 198152 | tf_op jit(solution)/shard_map/ppermute | solution.py:39
  148.1 9.6 %collective-permute-start.20 = (f32[129,128]{1,0:T(8,128)S(1)}, f32[129,128]{1,0:T(8,128)S(1)}, u32[]{:S(2)}, u32[]{:S(2)}) collective-permute-start(f32[129,128]{1,0:T(8,128)S(1)} %select_reduce_fusion.4), channel_id=1, source_target_pairs={{0,32},{4,36},{8,40},{12,44},{16,48},{20,52},{24,56},{28,60},{32,0... | collective-permute-start | bytes 198152 | tf_op jit(solution)/shard_map/ppermute | solution.py:28
  157.7 5.6 %collective-permute-start.21 = (f32[129,128]{1,0:T(8,128)S(1)}, f32[129,128]{1,0:T(8,128)S(1)}, u32[]{:S(2)}, u32[]{:S(2)}) collective-permute-start(f32[129,128]{1,0:T(8,128)S(1)} %add.218), channel_id=1, source_target_pairs={{0,64},{4,68},{8,72},{12,76},{16,80},{20,84},{24,88},{28,92},{32,9... | collective-permute-start | bytes 198152 | tf_op jit(solution)/shard_map/ppermute | solution.py:39
  157.8 6.8 %collective-permute-start.22 = (f32[129,128]{1,0:T(8,128)S(1)}, f32[129,128]{1,0:T(8,128)S(1)}, u32[]{:S(2)}, u32[]{:S(2)}) collective-permute-start(f32[129,128]{1,0:T(8,128)S(1)} %add.218), channel_id=1, source_target_pairs={{0,128},{4,132},{8,136},{12,140},{16,144},{20,148},{24,152},{28,15... | collective-permute-start | bytes 198152 | tf_op jit(solution)/shard_map/ppermute | solution.py:39
  167.0 6.0 %collective-permute-start.24 = (f32[128,128]{1,0:T(8,128)S(1)}, f32[128,128]{1,0:T(8,128)S(1)}, u32[]{:S(2)}, u32[]{:S(2)}) collective-permute-start(f32[128,128]{1,0:T(8,128)S(1)} %fusion.155), channel_id=1, source_target_pairs={{0,1},{1,2},{2,3},{3,0},{4,5},{5,6},{6,7},{7,4},{8,9},{9,10},{10,1... | collective-permute-start | bytes 196616 | tf_op jit(solution)/shard_map/ppermute | solution.py:39
  167.5 6.8 %collective-permute-start.25 = (f32[128,128]{1,0:T(8,128)S(1)}, f32[128,128]{1,0:T(8,128)S(1)}, u32[]{:S(2)}, u32[]{:S(2)}) collective-permute-start(f32[128,128]{1,0:T(8,128)S(1)} %fusion.155), channel_id=1, source_target_pairs={{0,2},{1,3},{2,0},{3,1},{4,6},{5,7},{6,4},{7,5},{8,10},{9,11},{10,... | collective-permute-start | bytes 196616 | tf_op jit(solution)/shard_map/ppermute | solution.py:39
  177.8 6.7 %collective-permute-start.29 = (f32[128,128]{1,0:T(8,128)S(1)}, f32[128,128]{1,0:T(8,128)S(1)}, u32[]{:S(2)}, u32[]{:S(2)}) collective-permute-start(f32[128,128]{1,0:T(8,128)S(1)} %add.219), channel_id=1, source_target_pairs={{0,16},{4,20},{8,24},{12,28},{16,0},{20,4},{24,8},{28,12},{32,48},... | collective-permute-start | bytes 196616 | tf_op jit(solution)/shard_map/ppermute | solution.py:39
  180.2 6.3 %collective-permute-start.30 = (f32[128,128]{1,0:T(8,128)S(1)}, f32[128,128]{1,0:T(8,128)S(1)}, u32[]{:S(2)}, u32[]{:S(2)}) collective-permute-start(f32[128,128]{1,0:T(8,128)S(1)} %add.219), channel_id=1, source_target_pairs={{0,24},{4,28},{8,0},{12,4},{16,8},{20,12},{24,16},{28,20},{32,56},... | collective-permute-start | bytes 196616 | tf_op jit(solution)/shard_map/ppermute | solution.py:39
  187.2 9.4 %collective-permute-start.31 = (f32[128,128]{1,0:T(8,128)S(1)}, f32[128,128]{1,0:T(8,128)S(1)}, u32[]{:S(2)}, u32[]{:S(2)}) collective-permute-start(f32[128,128]{1,0:T(8,128)S(1)} %select_reduce_fusion.10), channel_id=1, source_target_pairs={{0,32},{4,36},{8,40},{12,44},{16,48},{20,52},{24,56},{28,60},{32,0... | collective-permute-start | bytes 196616 | tf_op jit(solution)/shard_map/ppermute | solution.py:28
  196.7 5.6 %collective-permute-start.32 = (f32[128,128]{1,0:T(8,128)S(1)}, f32[128,128]{1,0:T(8,128)S(1)}, u32[]{:S(2)}, u32[]{:S(2)}) collective-permute-start(f32[128,128]{1,0:T(8,128)S(1)} %add.220), channel_id=1, source_target_pairs={{0,64},{4,68},{8,72},{12,76},{16,80},{20,84},{24,88},{28,92},{32,9... | collective-permute-start | bytes 196616 | tf_op jit(solution)/shard_map/ppermute | solution.py:39
  197.1 5.8 %collective-permute-start.33 = (f32[128,128]{1,0:T(8,128)S(1)}, f32[128,128]{1,0:T(8,128)S(1)}, u32[]{:S(2)}, u32[]{:S(2)}) collective-permute-start(f32[128,128]{1,0:T(8,128)S(1)} %add.220), channel_id=1, source_target_pairs={{0,128},{4,132},{8,136},{12,140},{16,144},{20,148},{24,152},{28,15... | collective-permute-start | bytes 196616 | tf_op jit(solution)/shard_map/ppermute | solution.py:39
  272.4 5.8 %collective-permute-start.39 = (f32[257,128]{1,0:T(8,128)S(1)}, f32[257,128]{1,0:T(8,128)S(1)}, u32[]{:S(2)}, u32[]{:S(2)}) collective-permute-start(f32[257,128]{1,0:T(8,128)S(1)} %get-tuple-element.32), channel_id=1, source_target_pairs={{0,3},{1,0},{2,1},{3,2},{4,7},{5,4},{6,5},{7,6},{8,11},{9,8},{10,9... | collective-permute-start | bytes 394760 | tf_op jit(solution)/shard_map/ppermute | solution.py:39
  273.7 7.7 %collective-permute-start.37 = (f32[257,128]{1,0:T(8,128)S(1)}, f32[257,128]{1,0:T(8,128)S(1)}, u32[]{:S(2)}, u32[]{:S(2)}) collective-permute-start(f32[257,128]{1,0:T(8,128)S(1)} %get-tuple-element.32), channel_id=1, source_target_pairs={{0,1},{1,2},{2,3},{3,0},{4,5},{5,6},{6,7},{7,4},{8,9},{9,10},{10,1... | collective-permute-start | bytes 394760 | tf_op jit(solution)/shard_map/ppermute | solution.py:39
  274.6 6.8 %collective-permute-start.38 = (f32[257,128]{1,0:T(8,128)S(1)}, f32[257,128]{1,0:T(8,128)S(1)}, u32[]{:S(2)}, u32[]{:S(2)}) collective-permute-start(f32[257,128]{1,0:T(8,128)S(1)} %get-tuple-element.32), channel_id=1, source_target_pairs={{0,2},{1,3},{2,0},{3,1},{4,6},{5,7},{6,4},{7,5},{8,10},{9,11},{10,... | collective-permute-start | bytes 394760 | tf_op jit(solution)/shard_map/ppermute | solution.py:39
  283.6 8.5 %collective-permute-start.41 = (f32[257,128]{1,0:T(8,128)S(1)}, f32[257,128]{1,0:T(8,128)S(1)}, u32[]{:S(2)}, u32[]{:S(2)}) collective-permute-start(f32[257,128]{1,0:T(8,128)S(1)} %add.229), channel_id=1, source_target_pairs={{0,8},{4,12},{8,16},{12,20},{16,24},{20,28},{24,0},{28,4},{32,40},... | collective-permute-start | bytes 394760 | tf_op jit(solution)/shard_map/ppermute | solution.py:39
  283.7 15.0 %collective-permute-start.42 = (f32[257,128]{1,0:T(8,128)S(1)}, f32[257,128]{1,0:T(8,128)S(1)}, u32[]{:S(2)}, u32[]{:S(2)}) collective-permute-start(f32[257,128]{1,0:T(8,128)S(1)} %add.229), channel_id=1, source_target_pairs={{0,16},{4,20},{8,24},{12,28},{16,0},{20,4},{24,8},{28,12},{32,48},... | collective-permute-start | bytes 394760 | tf_op jit(solution)/shard_map/ppermute | solution.py:39
  290.0 11.5 %collective-permute-start.43 = (f32[257,128]{1,0:T(8,128)S(1)}, f32[257,128]{1,0:T(8,128)S(1)}, u32[]{:S(2)}, u32[]{:S(2)}) collective-permute-start(f32[257,128]{1,0:T(8,128)S(1)} %add.229), channel_id=1, source_target_pairs={{0,24},{4,28},{8,0},{12,4},{16,8},{20,12},{24,16},{28,20},{32,56},... | collective-permute-start | bytes 394760 | tf_op jit(solution)/shard_map/ppermute | solution.py:39
  302.3 11.7 %collective-permute-start.44 = (f32[257,128]{1,0:T(8,128)S(1)}, f32[257,128]{1,0:T(8,128)S(1)}, u32[]{:S(2)}, u32[]{:S(2)}) collective-permute-start(f32[257,128]{1,0:T(8,128)S(1)} %select_reduce_fusion.1), channel_id=1, source_target_pairs={{0,32},{4,36},{8,40},{12,44},{16,48},{20,52},{24,56},{28,60},{32,0... | collective-permute-start | bytes 394760 | tf_op jit(solution)/shard_map/ppermute | solution.py:28
  314.0 9.5 %collective-permute-start.45 = (f32[257,128]{1,0:T(8,128)S(1)}, f32[257,128]{1,0:T(8,128)S(1)}, u32[]{:S(2)}, u32[]{:S(2)}) collective-permute-start(f32[257,128]{1,0:T(8,128)S(1)} %add.230), channel_id=1, source_target_pairs={{0,64},{4,68},{8,72},{12,76},{16,80},{20,84},{24,88},{28,92},{32,9... | collective-permute-start | bytes 394760 | tf_op jit(solution)/shard_map/ppermute | solution.py:39
  314.1 9.4 %collective-permute-start.46 = (f32[257,128]{1,0:T(8,128)S(1)}, f32[257,128]{1,0:T(8,128)S(1)}, u32[]{:S(2)}, u32[]{:S(2)}) collective-permute-start(f32[257,128]{1,0:T(8,128)S(1)} %add.230), channel_id=1, source_target_pairs={{0,128},{4,132},{8,136},{12,140},{16,144},{20,148},{24,152},{28,15... | collective-permute-start | bytes 394760 | tf_op jit(solution)/shard_map/ppermute | solution.py:39
  316.6 7.4 %collective-permute-start.47 = (f32[257,128]{1,0:T(8,128)S(1)}, f32[257,128]{1,0:T(8,128)S(1)}, u32[]{:S(2)}, u32[]{:S(2)}) collective-permute-start(f32[257,128]{1,0:T(8,128)S(1)} %add.230), channel_id=1, source_target_pairs={{0,192},{4,196},{8,200},{12,204},{16,208},{20,212},{24,216},{28,22... | collective-permute-start | bytes 394760 | tf_op jit(solution)/shard_map/ppermute | solution.py:39
  325.6 6.3 %collective-permute-start.48 = (f32[128,128]{1,0:T(8,128)S(1)}, f32[128,128]{1,0:T(8,128)S(1)}, u32[]{:S(2)}, u32[]{:S(2)}) collective-permute-start(f32[128,128]{1,0:T(8,128)S(1)} %fusion.156), channel_id=1, source_target_pairs={{0,1},{1,2},{2,3},{3,0},{4,5},{5,6},{6,7},{7,4},{8,9},{9,10},{10,1... | collective-permute-start | bytes 196616 | tf_op jit(solution)/shard_map/ppermute | solution.py:39
  325.7 6.2 %collective-permute-start.49 = (f32[128,128]{1,0:T(8,128)S(1)}, f32[128,128]{1,0:T(8,128)S(1)}, u32[]{:S(2)}, u32[]{:S(2)}) collective-permute-start(f32[128,128]{1,0:T(8,128)S(1)} %fusion.156), channel_id=1, source_target_pairs={{0,2},{1,3},{2,0},{3,1},{4,6},{5,7},{6,4},{7,5},{8,10},{9,11},{10,... | collective-permute-start | bytes 196616 | tf_op jit(solution)/shard_map/ppermute | solution.py:39
  334.8 6.2 %collective-permute-start.53 = (f32[128,128]{1,0:T(8,128)S(1)}, f32[128,128]{1,0:T(8,128)S(1)}, u32[]{:S(2)}, u32[]{:S(2)}) collective-permute-start(f32[128,128]{1,0:T(8,128)S(1)} %add.231), channel_id=1, source_target_pairs={{0,16},{4,20},{8,24},{12,28},{16,0},{20,4},{24,8},{28,12},{32,48},... | collective-permute-start | bytes 196616 | tf_op jit(solution)/shard_map/ppermute | solution.py:39
  334.9 7.8 %collective-permute-start.54 = (f32[128,128]{1,0:T(8,128)S(1)}, f32[128,128]{1,0:T(8,128)S(1)}, u32[]{:S(2)}, u32[]{:S(2)}) collective-permute-start(f32[128,128]{1,0:T(8,128)S(1)} %add.231), channel_id=1, source_target_pairs={{0,24},{4,28},{8,0},{12,4},{16,8},{20,12},{24,16},{28,20},{32,56},... | collective-permute-start | bytes 196616 | tf_op jit(solution)/shard_map/ppermute | solution.py:39
  343.5 8.7 %collective-permute-start.55 = (f32[128,128]{1,0:T(8,128)S(1)}, f32[128,128]{1,0:T(8,128)S(1)}, u32[]{:S(2)}, u32[]{:S(2)}) collective-permute-start(f32[128,128]{1,0:T(8,128)S(1)} %select_reduce_fusion.7), channel_id=1, source_target_pairs={{0,32},{4,36},{8,40},{12,44},{16,48},{20,52},{24,56},{28,60},{32,0... | collective-permute-start | bytes 196616 | tf_op jit(solution)/shard_map/ppermute | solution.py:28
  352.2 6.3 %collective-permute-start.56 = (f32[128,128]{1,0:T(8,128)S(1)}, f32[128,128]{1,0:T(8,128)S(1)}, u32[]{:S(2)}, u32[]{:S(2)}) collective-permute-start(f32[128,128]{1,0:T(8,128)S(1)} %add.232), channel_id=1, source_target_pairs={{0,64},{4,68},{8,72},{12,76},{16,80},{20,84},{24,88},{28,92},{32,9... | collective-permute-start | bytes 196616 | tf_op jit(solution)/shard_map/ppermute | solution.py:39
  353.1 6.6 %collective-permute-start.57 = (f32[128,128]{1,0:T(8,128)S(1)}, f32[128,128]{1,0:T(8,128)S(1)}, u32[]{:S(2)}, u32[]{:S(2)}) collective-permute-start(f32[128,128]{1,0:T(8,128)S(1)} %add.232), channel_id=1, source_target_pairs={{0,128},{4,132},{8,136},{12,140},{16,144},{20,148},{24,152},{28,15... | collective-permute-start | bytes 196616 | tf_op jit(solution)/shard_map/ppermute | solution.py:39
  401.8 7.5 %collective-permute-start.66 = (f32[128]{0:T(128)S(1)}, f32[128]{0:T(128)S(1)}, u32[]{:S(2)}, u32[]{:S(2)}) collective-permute-start(f32[128]{0:T(128)S(1)} %select_reduce_fusion.17), channel_id=1, source_target_pairs={{0,32},{4,36},{8,40},{12,44},{16,48},{20,52},{24,56},{28,60},{32,0... | collective-permute-start | bytes 1544 | tf_op jit(solution)/shard_map/ppermute | solution.py:28
  409.3 9.3 %collective-permute-start.67 = (f32[128]{0:T(128)S(1)}, f32[128]{0:T(128)S(1)}, u32[]{:S(2)}, u32[]{:S(2)}) collective-permute-start(f32[128]{0:T(128)S(1)} %add.234), channel_id=1, source_target_pairs={{0,64},{4,68},{8,72},{12,76},{16,80},{20,84},{24,88},{28,92},{32,9... | collective-permute-start | bytes 1544 | tf_op jit(solution)/shard_map/ppermute | solution.py:39
  409.5 9.1 %collective-permute-start.68 = (f32[128]{0:T(128)S(1)}, f32[128]{0:T(128)S(1)}, u32[]{:S(2)}, u32[]{:S(2)}) collective-permute-start(f32[128]{0:T(128)S(1)} %add.234), channel_id=1, source_target_pairs={{0,128},{4,132},{8,136},{12,140},{16,144},{20,148},{24,152},{28,15... | collective-permute-start | bytes 1544 | tf_op jit(solution)/shard_map/ppermute | solution.py:39
  412.2 6.5 %collective-permute-start.69 = (f32[128]{0:T(128)S(1)}, f32[128]{0:T(128)S(1)}, u32[]{:S(2)}, u32[]{:S(2)}) collective-permute-start(f32[128]{0:T(128)S(1)} %add.234), channel_id=1, source_target_pairs={{0,192},{4,196},{8,200},{12,204},{16,208},{20,212},{24,216},{28,22... | collective-permute-start | bytes 1544 | tf_op jit(solution)/shard_map/ppermute | solution.py:39
  415.2 10.1 %all-to-all-start.3 = ((bf16[4,2,16384]{2,1,0:T(2,128)(2,1)}), bf16[4,2,16384]{2,1,0:T(2,128)(2,1)S(1)}, u32[]{:S(2)}, u32[]{:S(2)}) async-start(bf16[4,2,16384]{2,1,0:T(2,128)(2,1)} %reshape.462), calls=%async_computation.3 | async-start | bytes 524288 | tf_op jit(solution)/shard_map/all_to_all | solution.py:145
  (38 other events, 183.3 us)
